TPU v7x, 256 devices: a whole 4x4x8 slice. The times are simulated.
256 devices in a mesh: section: 16 (over y, x), dp: 16 (over z, core).
Axes of the slice: x: 4, y: 4, z: 8, core: 2. Of those that a mesh axis runs over, the one named last changes fastest.
Arguments:
- hidden: bfloat16 [16, 256, 8192], P('dp', 'section'), may hold values from -1500 to 1500
- head: bfloat16 [65536, 8192], P('section', 'dp'), may hold values from -0.0625 to 0.0625
- block_id: int32 [16, 16], P(None, 'section'), may hold values from 0 to 7
- block_live: int32 [16, 16], P(None, 'section'), may hold values from 0 to 1, as said below
- teacher: bfloat16 [16, 256, 8192], P('dp', None, 'section'), may hold values from -400 to 400
Outputs:
- grad_hidden: bfloat16 [16, 256, 8192], P('dp', 'section')
- grad_head: bfloat16 [65536, 8192], P('section', 'dp')
Inputs may be any that keep to these rules, and one draw needn't show every extreme that they name: `block_live`: every micro-batch has at least one live section.
All inputs are finite; a program needn't handle non-finite values.
Results may differ from a plain program's by a relative error of at most 0.0056.
Values may be sent and summed in bfloat16 or wider, within the bound.
No kernel may reach another device: no remote copies, remote signals or barrier semaphores. Data moves between devices by JAX's collectives and lax.ppermute only.
A program may use at most 128 MiB of HBM per device.

v0:
```python
import jax
import jax.numpy as jnp
from jax import lax
from jax.sharding import PartitionSpec as P

neg_fill = -1e30


def local(hidden, head, block_id, block_live, teacher):
    my_replica = lax.axis_index("dp")
    n_dp = lax.axis_size("dp")
    tok_local = hidden.shape[1]
    model_width = hidden.shape[2]
    block_rows = teacher.shape[2]
    col_width = head.shape[1]
    blocks = head.shape[0] // block_rows
    table = head.reshape(blocks, block_rows, col_width)
    block_ids = block_id[:, 0]
    live_flags = block_live[:, 0]
    n_mb = block_ids.shape[0]
    pieces = hidden.reshape(1, tok_local, n_dp, col_width)
    pieces = lax.all_to_all(pieces, "dp", split_axis=2, concat_axis=0, tiled=True)
    hid_w = lax.all_gather(pieces, "section", axis=1, tiled=True).reshape(n_mb, -1, col_width)
    picked = jnp.take(table, block_ids, axis=0)
    part = jnp.einsum("mtw,mrw->mtr", hid_w, picked, preferred_element_type=jnp.float32)
    logits = lax.psum_scatter(part, "dp", scatter_dimension=0, tiled=True)[0]
    own_live = lax.dynamic_index_in_dim(live_flags, my_replica, 0, keepdims=False) > 0
    teach = teacher[0].astype(jnp.float32)
    live_value = jnp.where(own_live, 1.0, 0.0).astype(jnp.float32)
    stud_local = jnp.where(own_live, jnp.max(logits, axis=1), neg_fill)
    teach_local = jnp.where(own_live, jnp.max(teach, axis=1), neg_fill)
    stud_top, teach_top = lax.pmax((stud_local, teach_local), "section")
    stud_part = jnp.where(own_live, jnp.sum(jnp.exp(logits - stud_top[:, None]), axis=1), 0.0)
    teach_part = jnp.where(own_live, jnp.sum(jnp.exp(teach - teach_top[:, None]), axis=1), 0.0)
    stud_total, teach_total, live_count = lax.psum((stud_part, teach_part, live_value), "section")
    student = jnp.where(own_live, jnp.exp(logits - stud_top[:, None]) / stud_total[:, None], 0.0)
    teach_prob = jnp.where(
        own_live, jnp.exp(teach - teach_top[:, None]) / teach_total[:, None], 0.0
    )
    logit_grad = (block_rows * live_count * (student - teach_prob)).astype(jnp.bfloat16)
    grads = lax.all_gather(logit_grad[None], "dp", axis=0, tiled=True)
    contrib = jnp.einsum("mtr,mtw->mrw", grads, hid_w, preferred_element_type=jnp.float32).astype(
        jnp.bfloat16
    )
    block_range = jnp.arange(blocks, dtype=jnp.int32)[None, :]
    selector = jnp.where(
        (live_flags[:, None] > 0) & (block_ids[:, None] == block_range), 1.0, 0.0
    ).astype(jnp.bfloat16)
    grad_head = jnp.einsum("mb,mrw->brw", selector, contrib, preferred_element_type=jnp.float32)
    grad_head = grad_head.astype(jnp.bfloat16).reshape(blocks * block_rows, col_width)
    ghid = jnp.einsum("mtr,mrw->mtw", grads, picked, preferred_element_type=jnp.float32)
    ghid = lax.psum_scatter(ghid, "section", scatter_dimension=1, tiled=True).astype(jnp.bfloat16)
    ghid = lax.all_to_all(ghid, "dp", split_axis=0, concat_axis=2, tiled=True)
    grad_hidden = ghid.reshape(1, tok_local, model_width)
    return (grad_hidden, grad_head)


def solution(mesh):
    placed = (
        P("dp", "section", None),
        P("section", "dp"),
        P(None, "section"),
        P(None, "section"),
        P("dp", None, "section"),
    )
    return jax.shard_map(
        local,
        mesh=mesh,
        in_specs=placed,
        out_specs=(P("dp", "section", None), P("section", "dp")),
        check_vma=False,
    )
```

profile of v0, /device:TPU:1, one launch (start us, length us, event | category | flops | bytes accessed | tf_op | source)
XLA Modules:
  0.0 412.9 jit_solution(15351352990721341709)
XLA Ops:
  7.2 1.0 copy.29
  8.2 21.6 %all_to_all.36 = bf16[1,16,16,512]{3,1,0,2:T(8,128)(2,1)} all-to-all(bf16[1,16,16,512]{3,1,0,2:T(8,128)(2,1)S(1)} %bitcast.54), channel_id=1, replica_groups=mesh['section'=16,'dp'=16] {'dp'}, dimensions={2} | all-to-all | bytes 524288 | tf_op jit(solution)/shard_map/all_to_all | solution.py:22
  29.8 0.0 reduce-scatter.3.cloned.1.call-start
  29.8 0.7 fusion.34
  30.5 7.0 %gather_fusion = bf16[16,512,512]{2,1,0:T(8,128)(2,1)} fusion(bf16[8,512,512]{2,1,0:T(8,128)(2,1)} %bitcast.50, s32[1024]{0:T(1024)S(1)} %pad_clamp_fusion), kind=kCustom, calls=%fused_computation | custom fusion | bytes 16777280 | tf_op jit(solution)/shard_map/jit(_take)/gather | solution.py:24
  37.5 45.8 %all-gather.6.cloned.1.call-done = bf16[16,1,256,1,512]{4,2,0,3,1:T(8,128)(2,1)} async-done(((bf16[16,1,16,1,512]{4,2,0,3,1:T(8,128)(2,1)}), bf16[16,1,256,1,512]{4,2,0,3,1:T(8,128)(2,1)}) %all-gather.6.cloned.1.call-update) | async-done | bytes 4194320 | tf_op jit(solution)/shard_map/all_gather | solution.py:23
  83.3 10.2 %fusion.6 = f32[16,256,512]{1,2,0:T(8,128)} fusion(bf16[16,1,256,1,512]{4,2,0,3,1:T(8,128)(2,1)} %all-gather.6.cloned.1.call-done, bf16[16,512,512]{2,1,0:T(8,128)(2,1)} %gather_fusion, pred[16]{0:T(512)(128)(4,1)S(1)} %and_bitcast_fusion), kind=kOutput, calls=%fused_computation.9 | convolution fusion | flops 2151677952 | bytes 20971536 | tf_op jit(solution)/shard_map/mtw,mrw->mtr/dot_general | solution.py:25
  93.5 0.9 copy-done
  94.4 0.1 copy.15
  94.6 0.1 reduce_max.24
  94.7 0.6 fusion.35
  95.9 0.6 convert_select_fusion
  96.6 64.4 %reduce-scatter.3.cloned.1.call-done = f32[1,256,512]{1,2,0:T(8,128)} async-done(((f32[16,256,512]{1,2,0:T(8,128)}), f32[1,256,512]{1,2,0:T(8,128)}) %reduce-scatter.3.cloned.1.call-update) | async-done | bytes 524304 | tf_op jit(solution)/shard_map/reduce_scatter | solution.py:26
  161.0 1.1 reduce_max.23
  162.1 0.6 broadcast_select_fusion.7
  162.8 33.3 %all-reduce.1 = (f32[256]{0:T(256)S(1)}, f32[256]{0:T(256)S(1)}) all-reduce(f32[256]{0:T(256)S(1)} %convert_select_fusion, f32[256]{0:T(256)S(1)} %broadcast_select_fusion.7), channel_id=1, replica_groups=mesh['section'=16,'dp'=16] {'section'}, use_global_device_ids=true, to_apply=%region_7.8 | all-reduce | flops 512 | bytes 4096 | tf_op jit(solution)/shard_map/pmax | solution.py:32
  196.1 0.1 fusion.19
  196.2 1.2 fusion.21
  197.4 0.6 broadcast_select_fusion.5
  198.0 29.2 %all-reduce = (f32[256]{0:T(256)S(1)}, f32[256]{0:T(256)S(1)}, f32[]{:T(128)}) all-reduce(f32[256]{0:T(256)S(1)} %get-tuple-element.7, f32[256]{0:T(256)S(1)} %get-tuple-element.8, f32[]{:T(128)S(6)} %select_n.58), channel_id=1, replica_groups=mesh['section'=16,'dp'=16] {'section'}, use_global_device_ids=true, to_apply=%region_9.10 | all-reduce | flops 513 | bytes 4104 | tf_op jit(solution)/shard_map/psum | solution.py:35
  227.9 1.9 fusion.22
  229.8 0.8 copy.16
  230.7 54.8 %all-gather.4.cloned.1.call-done = bf16[16,256,512]{2,1,0:T(8,128)(2,1)} async-done(((bf16[1,256,512]{2,1,0:T(8,128)(2,1)}), bf16[16,256,512]{2,1,0:T(8,128)(2,1)}) %all-gather.4.cloned.1.call-update) | async-done | bytes 4194320 | tf_op jit(solution)/shard_map/all_gather | solution.py:41
  285.5 10.3 %fusion.5 = f32[16,256,512]{2,1,0:T(8,128)} fusion(bf16[16,256,512]{2,1,0:T(8,128)(2,1)} %all-gather.4.cloned.1.call-done, bf16[16,512,512]{2,1,0:T(8,128)(2,1)} %gather_fusion, pred[16]{0:T(512)(128)(4,1)S(1)} %and_bitcast_fusion), kind=kOutput, calls=%fused_computation.8 | convolution fusion | flops 2151677952 | bytes 20971536 | tf_op jit(solution)/shard_map/mtr,mrw->mtw/dot_general | solution.py:51
  295.8 9.1 %convolution_convert_fusion = bf16[16,512,512]{2,1,0:T(8,128)(2,1)} fusion(bf16[16,256,512]{2,1,0:T(8,128)(2,1)} %all-gather.4.cloned.1.call-done, bf16[16,1,256,1,512]{4,2,0,3,1:T(8,128)(2,1)} %all-gather.6.cloned.1.call-done), kind=kOutput, calls=%fused_computation.4 | convolution fusion | flops 2151677952 | bytes 16777216 | tf_op jit(solution)/shard_map/mtr,mtw->mrw/dot_general | solution.py:42
  304.9 78.3 %reduce-scatter.5.cloned.1.call-done = f32[16,16,512]{2,1,0:T(8,128)} async-done(((f32[16,256,512]{2,1,0:T(8,128)}), f32[16,16,512]{2,1,0:T(8,128)}) %reduce-scatter.5.cloned.1.call-update) | async-done | bytes 524304 | tf_op jit(solution)/shard_map/reduce_scatter | solution.py:52
  383.2 1.8 convert_element_type.29
  385.0 9.0 %all-to-all-start.1 = ((bf16[16,16,512]{2,1,0:T(8,128)(2,1)}), bf16[16,16,512]{2,1,0:T(8,128)(2,1)S(1)}, u32[]{:S(2)}, u32[]{:S(2)}) async-start(bf16[16,16,512]{2,1,0:T(8,128)(2,1)} %convert_element_type.29), calls=%async_computation.3 | async-start | bytes 524288 | tf_op jit(solution)/shard_map/all_to_all | solution.py:53
  393.9 8.1 %fusion.9 = bf16[8,512,512]{2,0,1:T(8,128)(2,1)S(1)} fusion(bf16[16,512,512]{2,1,0:T(8,128)(2,1)} %convolution_convert_fusion, s32[16]{0:T(128)S(1)} %bitcast.57, pred[16]{0:T(512)(128)(4,1)S(1)} %compare_bitcast_fusion), kind=kOutput, calls=%fused_computation.10 | convolution fusion | flops 69206528 | bytes 12582992 | tf_op jit(solution)/shard_map/mb,mrw->brw/dot_general | solution.py:49
  402.0 3.5 copy.20
  405.5 0.1 all-to-all-done.1
  405.6 0.7 copy.23
  (15 shorter events, 0.2 us)
Async XLA Ops:
  7.2 76.1 %all-gather.6.cloned.1.call-start = ((), (), s32[]{:S(2)}) async-start(), calls=%async_computation.7 | async-start | bytes 4456448 | tf_op jit(solution)/shard_map/all_gather | solution.py:23
  29.8 131.2 %reduce-scatter.3.cloned.1.call-start = ((), (), s32[]{:S(2)}) async-start(), calls=%async_computation.4 | async-start | bytes 8912896 | tf_op jit(solution)/shard_map/reduce_scatter | solution.py:26
  30.5 7.0 %copy-start.1 = (s32[16,1]{0,1:T(1,128)S(1)}, s32[16,1]{0,1:T(1,128)}, u32[]{:S(2)}) copy-start(s32[16,1]{0,1:T(1,128)} %param.7) | copy-start | bytes 196
  93.5 0.9 copy-start
  93.5 1.2 copy-start.2
  93.5 192.0 %all-gather.4.cloned.1.call-start = ((), (), s32[]{:S(2)}) async-start(), calls=%async_computation.5 | async-start | bytes 4456448 | tf_op jit(solution)/shard_map/all_gather | solution.py:41
  230.7 152.5 %reduce-scatter.5.cloned.1.call-start = ((), (), s32[]{:S(2)}) async-start(), calls=%async_computation.6 | async-start | bytes 8912896 | tf_op jit(solution)/shard_map/reduce_scatter | solution.py:52
  385.0 20.7 %all-to-all-start.1 = ((bf16[16,16,512]{2,1,0:T(8,128)(2,1)}), bf16[16,16,512]{2,1,0:T(8,128)(2,1)S(1)}, u32[]{:S(2)}, u32[]{:S(2)}) async-start(bf16[16,16,512]{2,1,0:T(8,128)(2,1)} %convert_element_type.29), calls=%async_computation.3 | async-start | bytes 524288 | tf_op jit(solution)/shard_map/all_to_all | solution.py:53
Sparse Core Ops, SparseCore 0:
  29.9 53.3 all-gather.5
  93.6 67.3 reduce-scatter.2
  230.8 54.6 all-gather.3
  295.9 87.1 reduce-scatter.4
where the time goes:
time: 413 us
  waiting for transfers between devices  243 us (59%)
  blocking collectives  84.1 us (20%)
  matrix products  37.7 us (9%)
  between operations  15.1 us (4%)
  local copies, waits for them, and re-layouts  14 us (3%)
  other arithmetic  9.45 us (2%)
  starting transfers between devices  9.12 us (2%)
    reduce_scatter x1, waiting for transfers between devices, local(): lax.psum_scatter(ghid, 'section', scatter_dimension=1, tiled=True)  78.3 us
    reduce_scatter x1, waiting for transfers between devices, local(): logits = lax.psum_scatter(part, 'dp', scatter_dimension=0, tiled=True)[0]  64.4 us
    all_gather x1, waiting for transfers between devices, local(): grads = lax.all_gather(logit_grad[None], 'dp', axis=0, tiled=True)  54.8 us
    all_gather x1, waiting for transfers between devices, local(): lax.all_gather(pieces, 'section', axis=1, tiled=True)  45.8 us
    pmax x1, blocking collectives, local(): stud_top, teach_top = lax.pmax((stud_local, teach_local), 'section')  33.3 us
    psum x1, blocking collectives, local(): lax.psum((stud_part, teach_part, live_value), 'section')  29.2 us
    all_to_all x1, blocking collectives, local(): lax.all_to_all(pieces, 'dp', split_axis=2, concat_axis=0, tiled=True)  21.6 us
    dot_general x1, matrix products, local(): jnp.einsum('mtr,mrw->mtw', grads, picked, preferred_element_type=jnp.floa...  10.3 us
  transfers between devices with their start and end apart: 5, of which 5 were waited for; matrix products, arithmetic and copies ran while one was open for 7% of the time, Pallas kernels for 0%

commit v1 on v0

--- a/solution.py
+++ b/solution.py
@@ -1,9 +1,26 @@
+import functools
 import jax
 import jax.numpy as jnp
 from jax import lax
 from jax.sharding import PartitionSpec as P
 
 neg_fill = -1e30
+
+
+def remake_spans(tile_in, peer_axis, ndim_at):
+    long_array = jnp.concatenate(
+        lax.all_to_all(
+            jnp.stack([tile_in for _ in range(lax.axis_size(peer_axis))]),
+            axis_name=peer_axis,
+            split_axis=0,
+            concat_axis=0,
+        ),
+        axis=ndim_at,
+    )
+    return long_array
+
+
+_define_stops_all = functools.partial(remake_spans, peer_axis="section", ndim_at=1)
 
 
 def local(hidden, head, block_id, block_live, teacher):
@@ -20,7 +37,7 @@
     n_mb = block_ids.shape[0]
     pieces = hidden.reshape(1, tok_local, n_dp, col_width)
     pieces = lax.all_to_all(pieces, "dp", split_axis=2, concat_axis=0, tiled=True)
-    hid_w = lax.all_gather(pieces, "section", axis=1, tiled=True).reshape(n_mb, -1, col_width)
+    hid_w = _define_stops_all(pieces).reshape(n_mb, -1, col_width)
     picked = jnp.take(table, block_ids, axis=0)
     part = jnp.einsum("mtw,mrw->mtr", hid_w, picked, preferred_element_type=jnp.float32)
     logits = lax.psum_scatter(part, "dp", scatter_dimension=0, tiled=True)[0]

time: 413 us -> 431 us (1.044)
  local copies, waits for them, and re-layouts: 14 us -> 21.1 us
  starting transfers between devices: 9.12 us -> 15.8 us
  waiting for transfers between devices: 243 us -> 249 us
    all_to_all x0 -> x1, waiting for transfers between devices: none -> 58.4 us  [remake_spans(): lax.all_to_all(jnp.stack([tile_in for _ in range(lax.axis_size(peer_axis)...]
    all_gather x1 -> x0, waiting for transfers between devices: 45.8 us -> none  [local(): lax.all_gather(pieces, 'section', axis=1, tiled=True)]
    all_to_all x0 -> x1, starting transfers between devices: none -> 6.81 us  [remake_spans(): lax.all_to_all(jnp.stack([tile_in for _ in range(lax.axis_size(peer_axis)...]
    reduce_scatter x1, waiting for transfers between devices: 64.4 us -> 57.9 us  [local(): logits = lax.psum_scatter(part, 'dp', scatter_dimension=0, tiled=True)[0]]
where the time goes in v1:
time: 431 us
  waiting for transfers between devices  249 us (58%)
  blocking collectives  83.8 us (19%)
  matrix products  36.5 us (8%)
  local copies, waits for them, and re-layouts  21.1 us (5%)
  starting transfers between devices  15.8 us (4%)
  between operations  15.1 us (4%)
  other arithmetic  8.79 us (2%)
    reduce_scatter x1, waiting for transfers between devices, local(): lax.psum_scatter(ghid, 'section', scatter_dimension=1, tiled=True)  78.1 us
    all_to_all x1, waiting for transfers between devices, remake_spans(): lax.all_to_all(jnp.stack([tile_in for _ in range(lax.axis_size(peer_axis)...  58.4 us
    reduce_scatter x1, waiting for transfers between devices, local(): logits = lax.psum_scatter(part, 'dp', scatter_dimension=0, tiled=True)[0]  57.9 us
    all_gather x1, waiting for transfers between devices, local(): grads = lax.all_gather(logit_grad[None], 'dp', axis=0, tiled=True)  54.7 us
    pmax x1, blocking collectives, local(): stud_top, teach_top = lax.pmax((stud_local, teach_local), 'section')  33.2 us
    psum x1, blocking collectives, local(): lax.psum((stud_part, teach_part, live_value), 'section')  29.2 us
    all_to_all x1, blocking collectives, local(): lax.all_to_all(pieces, 'dp', split_axis=2, concat_axis=0, tiled=True)  21.5 us
    dot_general x1, matrix products, local(): jnp.einsum('mtr,mrw->mtw', grads, picked, preferred_element_type=jnp.floa...  10.3 us
  transfers between devices with their start and end apart: 5, of which 5 were waited for; matrix products, arithmetic and copies ran while one was open for 7% of the time, Pallas kernels for 0%

profile of v1, /device:TPU:1, one launch (start us, length us, event | category | flops | bytes accessed | tf_op | source)
XLA Modules:
  0.0 430.5 jit_solution(11105436985759427691)
XLA Ops:
  7.2 1.0 copy.38
  8.2 21.5 %all_to_all.38 = bf16[1,16,16,512]{3,1,0,2:T(8,128)(2,1)S(1)} all-to-all(bf16[1,16,16,512]{3,1,0,2:T(8,128)(2,1)S(1)} %bitcast.55), channel_id=1, replica_groups=mesh['section'=16,'dp'=16] {'dp'}, dimensions={2} | all-to-all | bytes 524288 | tf_op jit(solution)/shard_map/all_to_all | solution.py:39
  29.6 2.5 stack.5
  32.2 6.8 %all-to-all-start.1 = ((bf16[16,16,16,1,512]{4,2,1,3,0:T(8,128)(2,1)}), bf16[16,16,16,1,512]{4,2,1,3,0:T(8,128)(2,1)}, u32[]{:S(2)}, u32[]{:S(2)}) async-start(bf16[16,16,16,1,512]{4,2,1,3,0:T(8,128)(2,1)} %stack.5), calls=%async_computation.1 | async-start | bytes 8388608 | tf_op jit(solution)/shard_map/all_to_all | solution.py:12
  39.1 7.0 %gather_fusion = bf16[16,512,512]{2,1,0:T(8,128)(2,1)} fusion(bf16[8,512,512]{2,1,0:T(8,128)(2,1)} %bitcast.49, s32[1024]{0:T(1024)S(1)} %pad_clamp_fusion), kind=kCustom, calls=%fused_computation | custom fusion | bytes 16777280 | tf_op jit(solution)/shard_map/jit(_take)/gather | solution.py:41
  46.0 58.4 %all-to-all-done.1 = bf16[16,16,16,1,512]{4,2,1,3,0:T(8,128)(2,1)} async-done(((bf16[16,16,16,1,512]{4,2,1,3,0:T(8,128)(2,1)}), bf16[16,16,16,1,512]{4,2,1,3,0:T(8,128)(2,1)}, u32[]{:S(2)}, u32[]{:S(2)}) %all-to-all-start.1) | async-done | bytes 4194336 | tf_op jit(solution)/shard_map/all_to_all | solution.py:12
  104.4 2.6 copy.23
  107.1 2.0 copy-done
  109.1 9.0 %fusion.4 = f32[16,256,512]{1,2,0:T(8,128)} fusion(bf16[16,256,512]{2,1,0:T(8,128)(2,1)S(1)} %bitcast.50, bf16[16,512,512]{2,1,0:T(8,128)(2,1)} %gather_fusion, pred[16]{0:T(512)(128)(4,1)S(1)} %and_bitcast_fusion), kind=kOutput, calls=%fused_computation.7 | convolution fusion | flops 2151677952 | bytes 20971536 | tf_op jit(solution)/shard_map/mtw,mrw->mtr/dot_general | solution.py:42
  118.2 0.9 copy-done.1
  119.1 0.1 copy.24
  119.3 0.6 fusion.31
  120.6 0.6 convert_select_fusion
  121.2 57.9 %reduce-scatter.3.cloned.1.call-done = f32[1,256,512]{1,2,0:T(8,128)} async-done(((f32[16,256,512]{1,2,0:T(8,128)}), f32[1,256,512]{1,2,0:T(8,128)}) %reduce-scatter.3.cloned.1.call-update) | async-done | bytes 524304 | tf_op jit(solution)/shard_map/reduce_scatter | solution.py:43
  179.1 1.1 reduce_max.23
  180.3 0.6 broadcast_select_fusion.7
  180.9 33.2 %all-reduce.1 = (f32[256]{0:T(256)S(1)}, f32[256]{0:T(256)S(1)}) all-reduce(f32[256]{0:T(256)S(1)} %convert_select_fusion, f32[256]{0:T(256)S(1)} %broadcast_select_fusion.7), channel_id=1, replica_groups=mesh['section'=16,'dp'=16] {'section'}, use_global_device_ids=true, to_apply=%region_7.8 | all-reduce | flops 512 | bytes 4096 | tf_op jit(solution)/shard_map/pmax | solution.py:49
  214.2 1.2 fusion.17
  215.4 0.6 broadcast_select_fusion.5
  216.0 29.2 %all-reduce = (f32[256]{0:T(256)S(1)}, f32[256]{0:T(256)S(1)}, f32[]{:T(128)}) all-reduce(f32[256]{0:T(256)S(1)} %get-tuple-element.7, f32[256]{0:T(256)S(1)} %get-tuple-element.8, f32[]{:T(128)S(6)} %select_n.58), channel_id=1, replica_groups=mesh['section'=16,'dp'=16] {'section'}, use_global_device_ids=true, to_apply=%region_9.10 | all-reduce | flops 513 | bytes 4104 | tf_op jit(solution)/shard_map/psum | solution.py:52
  245.8 1.9 fusion.18
  247.7 0.8 copy.25
  248.6 54.7 %all-gather.2.cloned.1.call-done = bf16[16,256,512]{2,1,0:T(8,128)(2,1)} async-done(((bf16[1,256,512]{2,1,0:T(8,128)(2,1)}), bf16[16,256,512]{2,1,0:T(8,128)(2,1)}) %all-gather.2.cloned.1.call-update) | async-done | bytes 4194320 | tf_op jit(solution)/shard_map/all_gather | solution.py:58
  303.4 10.3 %fusion.2 = f32[16,256,512]{2,1,0:T(8,128)} fusion(bf16[16,256,512]{2,1,0:T(8,128)(2,1)} %all-gather.2.cloned.1.call-done, bf16[16,512,512]{2,1,0:T(8,128)(2,1)} %gather_fusion, pred[16]{0:T(512)(128)(4,1)S(1)} %and_bitcast_fusion), kind=kOutput, calls=%fused_computation.5 | convolution fusion | flops 2151677952 | bytes 20971536 | tf_op jit(solution)/shard_map/mtr,mrw->mtw/dot_general | solution.py:68
  313.7 9.1 %convolution_convert_fusion = bf16[16,512,512]{2,1,0:T(8,128)(2,1)} fusion(bf16[16,256,512]{2,1,0:T(8,128)(2,1)} %all-gather.2.cloned.1.call-done, bf16[16,256,512]{2,1,0:T(8,128)(2,1)} %bitcast.51), kind=kOutput, calls=%fused_computation.4 | convolution fusion | flops 2151677952 | bytes 16777216 | tf_op jit(solution)/shard_map/mtr,mtw->mrw/dot_general | solution.py:59
  322.8 78.1 %reduce-scatter.5.cloned.1.call-done = f32[16,16,512]{2,1,0:T(8,128)} async-done(((f32[16,256,512]{2,1,0:T(8,128)}), f32[16,16,512]{2,1,0:T(8,128)}) %reduce-scatter.5.cloned.1.call-update) | async-done | bytes 524304 | tf_op jit(solution)/shard_map/reduce_scatter | solution.py:69
  400.9 1.8 convert_element_type.29
  402.7 8.9 %all-to-all-start.2 = ((bf16[16,16,512]{2,1,0:T(8,128)(2,1)}), bf16[16,16,512]{2,1,0:T(8,128)(2,1)S(1)}, u32[]{:S(2)}, u32[]{:S(2)}) async-start(bf16[16,16,512]{2,1,0:T(8,128)(2,1)} %convert_element_type.29), calls=%async_computation.4 | async-start | bytes 524288 | tf_op jit(solution)/shard_map/all_to_all | solution.py:70
  411.6 8.1 %fusion.5 = bf16[8,512,512]{2,0,1:T(8,128)(2,1)S(1)} fusion(bf16[16,512,512]{2,1,0:T(8,128)(2,1)} %convolution_convert_fusion, s32[16]{0:T(128)S(1)} %bitcast.58, pred[16]{0:T(512)(128)(4,1)S(1)} %compare_bitcast_fusion), kind=kOutput, calls=%fused_computation.8 | convolution fusion | flops 69206528 | bytes 12582992 | tf_op jit(solution)/shard_map/mb,mrw->brw/dot_general | solution.py:66
  419.7 3.5 copy.29
  423.2 0.1 all-to-all-done.2
  423.3 0.7 copy.32
  (18 shorter events, 0.5 us)
Async XLA Ops:
  7.2 31.9 %copy-start.2 = (s32[16,1]{0,1:T(1,128)S(1)}, s32[16,1]{0,1:T(1,128)}, u32[]{:S(2)}) copy-start(s32[16,1]{0,1:T(1,128)} %param.7) | copy-start | bytes 196
  32.2 72.2 %all-to-all-start.1 = ((bf16[16,16,16,1,512]{4,2,1,3,0:T(8,128)(2,1)}), bf16[16,16,16,1,512]{4,2,1,3,0:T(8,128)(2,1)}, u32[]{:S(2)}, u32[]{:S(2)}) async-start(bf16[16,16,16,1,512]{4,2,1,3,0:T(8,128)(2,1)} %stack.5), calls=%async_computation.1 | async-start | bytes 8388608 | tf_op jit(solution)/shard_map/all_to_all | solution.py:12
  39.0 140.1 %reduce-scatter.3.cloned.1.call-start = ((), (), s32[]{:S(2)}) async-start(), calls=%async_computation.5 | async-start | bytes 8912896 | tf_op jit(solution)/shard_map/reduce_scatter | solution.py:43
  107.1 2.0 copy-start
  118.1 0.9 copy-start.1
  118.1 1.2 copy-start.3
  118.1 185.2 %all-gather.2.cloned.1.call-start = ((), (), s32[]{:S(2)}) async-start(), calls=%async_computation.6 | async-start | bytes 4456448 | tf_op jit(solution)/shard_map/all_gather | solution.py:58
  248.6 152.3 %reduce-scatter.5.cloned.1.call-start = ((), (), s32[]{:S(2)}) async-start(), calls=%async_computation.7 | async-start | bytes 8912896 | tf_op jit(solution)/shard_map/reduce_scatter | solution.py:69
  402.7 20.6 %all-to-all-start.2 = ((bf16[16,16,512]{2,1,0:T(8,128)(2,1)}), bf16[16,16,512]{2,1,0:T(8,128)(2,1)S(1)}, u32[]{:S(2)}, u32[]{:S(2)}) async-start(bf16[16,16,512]{2,1,0:T(8,128)(2,1)} %convert_element_type.29), calls=%async_computation.4 | async-start | bytes 524288 | tf_op jit(solution)/shard_map/all_to_all | solution.py:70
Sparse Core Ops, SparseCore 0:
  118.3 60.8 reduce-scatter.2
  248.7 54.5 all-gather.1
  313.8 87.0 reduce-scatter.4
